TPU v7x, 512 devices: a whole 4x8x8 slice. The times are simulated.
512 devices in a mesh: prompt: 32 (over x, y), sample: 16 (over z, core).
Axes of the slice: x: 4, y: 8, z: 8, core: 2. Of those that a mesh axis runs over, the one named last changes fastest.
Arguments:
- queries: bfloat16 [32, 16, 4, 8192], P('prompt', 'sample'), may hold values from -24 to 24
- new_kv: bfloat16 [32, 16, 4, 2, 1024], P('prompt', 'sample'), may hold values from -24 to 24
- suffix_kv: bfloat16 [32, 16, 256, 2, 1024], P('prompt', 'sample'), may hold values from -24 to 24
- suffix_len: int32 [32, 16], P('prompt', 'sample'), may hold values from 1 to 256, as said below
- prefix_head: bfloat16 [32, 2048, 2, 1024], P('prompt', 'sample'), may hold values from -24 to 24
- prefix_tail: bfloat16 [32, 2048, 2, 1024], P('prompt', 'sample'), may hold values from -24 to 24
- prefix_len: int32 [32], replicated, may hold values from 1024 to 4096, as said below
Outputs:
- attended: bfloat16 [32, 16, 4, 8192], P('prompt', 'sample')
Inputs may be any that keep to these rules, and one draw needn't show every extreme that they name: `suffix_len`: some sample has all 256 slots live and some only one. `prefix_len`: some prompt has all 4096 positions live and some only 1024.
All inputs are finite; a program needn't handle non-finite values.
Results may differ from a plain program's by a relative error of at most 0.001.
Values may be sent and summed in bfloat16 or wider, within the bound.
No kernel may reach another device: no remote copies, remote signals or barrier semaphores. Data moves between devices by JAX's collectives and lax.ppermute only.
A program may use at most 64 MiB of HBM per device.

v0:
```python
import jax
import jax.numpy as jnp
from jax import lax
from jax.sharding import PartitionSpec as P

QH = 64
KVH = 8
HEAD_SIZE = 128
NEG = -1e30


def from_behind(value, axis, steps):
    count = lax.axis_size(axis)
    pairs = [(source, (source + steps) % count) for source in range(count)]
    return lax.ppermute(value, axis, pairs)


def apply_weights(logit_scores, valid_mask, value_matrix, form):
    masked = jnp.where(valid_mask, logit_scores, NEG)
    maxima = jnp.max(masked, axis=-1)
    weights = jnp.where(valid_mask, jnp.exp(masked - maxima[..., None]), 0.0)
    totals = jnp.sum(weights, axis=-1)
    numerator = jnp.einsum(form, weights, value_matrix, precision=lax.Precision.HIGHEST)
    leading = numerator.shape[:2]
    return (
        numerator.reshape(leading + (QH, HEAD_SIZE)),
        maxima.reshape(leading + (QH,)),
        totals.reshape(leading + (QH,)),
    )


def prefix_terms(query_rows, pairs, start, length):
    sample_count, step_count = (query_rows.shape[0], query_rows.shape[1])
    block_len = pairs.shape[0]
    grouped_queries = query_rows.reshape(sample_count, step_count, KVH, QH // KVH, HEAD_SIZE)
    key_matrix = pairs[:, 0].reshape(block_len, KVH, HEAD_SIZE)
    value_matrix = pairs[:, 1].reshape(block_len, KVH, HEAD_SIZE).astype(jnp.float32)
    logit_scores = jnp.einsum(
        "rhlxf,vlf->rhlxv", grouped_queries, key_matrix, preferred_element_type=jnp.float32
    ) * HEAD_SIZE ** (-0.5)
    valid_mask = start + jnp.arange(block_len, dtype=jnp.int32) < length
    return apply_weights(logit_scores, valid_mask, value_matrix, "urpyj,jpi->urpyi")


def suffix_terms(query_rows, cache, fresh, length):
    sample_count, step_count = (query_rows.shape[0], query_rows.shape[1])
    slots = cache.shape[1]
    joined = jnp.concatenate([cache, fresh], axis=1)
    total_len = joined.shape[1]
    grouped_queries = query_rows.reshape(sample_count, step_count, KVH, QH // KVH, HEAD_SIZE)
    key_matrix = joined[:, :, 0].reshape(sample_count, total_len, KVH, HEAD_SIZE)
    value_matrix = (
        joined[:, :, 1].reshape(sample_count, total_len, KVH, HEAD_SIZE).astype(jnp.float32)
    )
    logit_scores = jnp.einsum(
        "stkgd,slkd->stkgl", grouped_queries, key_matrix, preferred_element_type=jnp.float32
    ) * HEAD_SIZE ** (-0.5)
    cache_live = jnp.arange(slots, dtype=jnp.int32)[None, :] < length[:, None]
    steps_live = (
        jnp.arange(step_count, dtype=jnp.int32)[None, :]
        <= jnp.arange(step_count, dtype=jnp.int32)[:, None]
    )
    valid_mask = jnp.concatenate(
        [
            jnp.broadcast_to(cache_live[:, None, :], (sample_count, step_count, slots)),
            steps_live[None],
        ],
        axis=2,
    )
    return apply_weights(
        logit_scores, valid_mask[:, :, None, None, :], value_matrix, "stkgl,slkd->stkgd"
    )


def join(former, latter):
    maxima = jnp.maximum(former[1], latter[1])
    scale_a = jnp.exp(former[1] - maxima)
    scale_b = jnp.exp(latter[1] - maxima)
    return (
        former[0] * scale_a[..., None] + latter[0] * scale_b[..., None],
        maxima,
        former[2] * scale_a + latter[2] * scale_b,
    )


def settle(stacked):
    maxima = jnp.max(stacked[1], axis=0)
    factors = jnp.exp(stacked[1] - maxima[None])
    return (
        jnp.sum(stacked[0] * factors[..., None], axis=0),
        maxima,
        jnp.sum(stacked[2] * factors, axis=0),
    )


def spread(partial_sums):
    return (
        lax.all_to_all(partial_sums[0][None], "sample", split_axis=1, concat_axis=0, tiled=True),
        lax.all_to_all(partial_sums[1][None], "sample", split_axis=1, concat_axis=0, tiled=True),
        lax.all_to_all(partial_sums[2][None], "sample", split_axis=1, concat_axis=0, tiled=True),
    )


def per_device(queries, new_kv, suffix_kv, suffix_len, prefix_head, prefix_tail, prefix_len):
    sample_count = lax.axis_size("sample")
    prompt_row = lax.axis_index("prompt")
    sample_slot = lax.axis_index("sample")
    block_len = prefix_head.shape[1]
    half_len = block_len * sample_count
    own_length = prefix_len[prompt_row]
    local_rows = queries[0]
    every_rows = lax.all_gather(queries, "sample", axis=1, tiled=True)[0]
    near_part = suffix_terms(local_rows, suffix_kv[0], new_kv[0], suffix_len[0])
    moved = from_behind(prefix_tail, "prompt", -1)
    own_part = prefix_terms(every_rows, prefix_head[0], sample_slot * block_len, own_length)
    tail_part = prefix_terms(every_rows, moved[0], half_len + sample_slot * block_len, own_length)
    result = join(settle(spread(join(own_part, tail_part))), near_part)
    attended = (result[0] / result[2][..., None]).astype(jnp.bfloat16)
    return attended.reshape(queries.shape)


def solution(mesh):
    in_specs = (
        P("prompt", "sample", None, None),
        P("prompt", "sample", None, None, None),
        P("prompt", "sample", None, None, None),
        P("prompt", "sample"),
        P("prompt", "sample", None, None),
        P("prompt", "sample", None, None),
        P(),
    )
    out_specs = P("prompt", "sample", None, None)
    return jax.shard_map(
        per_device, mesh=mesh, in_specs=in_specs, out_specs=out_specs, check_vma=False
    )
```

profile of v0, /device:TPU:1, one launch (start us, length us, event | category | flops | bytes accessed | tf_op | source)
XLA Modules:
  0.0 154.0 jit_solution(10899200841303403284)
XLA Ops:
  6.5 0.7 all-gather.2.cloned.1.call-update
  7.3 1.4 copy.107
  8.6 8.1 %collective-permute-start = (bf16[1,128,2,1024]{1,3,2,0:T(8,128)(2,1)S(1)}, bf16[1,128,2,1024]{1,3,2,0:T(8,128)(2,1)S(1)}, u32[]{:S(2)}, u32[]{:S(2)}) collective-permute-start(bf16[1,128,2,1024]{1,3,2,0:T(8,128)(2,1)S(1)} %copy.107), channel_id=1, source_target_pairs={{0,496},{16,0},{32,16},{48,32},{64,48},{80,64},{96,80},{112,96},{1... | collective-permute-start | bytes 1572872 | tf_op jit(solution)/shard_map/ppermute | solution.py:15
  16.8 1.4 copy.98
  20.1 7.2 %collective-permute-done = bf16[1,128,2,1024]{1,3,2,0:T(8,128)(2,1)S(1)} collective-permute-done((bf16[1,128,2,1024]{1,3,2,0:T(8,128)(2,1)S(1)}, bf16[1,128,2,1024]{1,3,2,0:T(8,128)(2,1)S(1)}, u32[]{:S(2)}, u32[]{:S(2)}) %collective-permute-start) | collective-permute-done | bytes 524320 | tf_op jit(solution)/shard_map/ppermute | solution.py:15
  27.4 30.0 %all-gather.2.cloned.1.call-done = bf16[1,16,4,8192]{3,2,0,1:T(4,128)(2,1)} async-done(((bf16[1,1,4,8192]{3,2,0,1:T(4,128)(2,1)}), bf16[1,16,4,8192]{3,2,0,1:T(4,128)(2,1)}) %all-gather.2.cloned.1.call-update) | async-done | bytes 1048592 | tf_op jit(solution)/shard_map/all_gather | solution.py:112
  57.4 2.1 %reshape.433 = bf16[16,4,8,8,128]{4,3,2,1,0:T(8,128)(2,1)S(1)} reshape(bf16[1,16,4,8192]{3,2,0,1:T(4,128)(2,1)} %all-gather.2.cloned.1.call-done) | data formatting | bytes 2097152 | tf_op jit(solution)/shard_map/reshape;squeeze | solution.py:35
  59.5 1.0 bitcast_reduce_fusion
  60.6 1.0 bitcast_reduce_fusion.1
  61.6 3.3 %fusion.47 = (f32[16,4,8,8]{0,3,1,2:T(8,128)S(1)}, f32[16,4,8,8,128]{4,0,3,1,2:T(8,128)}, f32[16,4,8,8]{0,3,1,2:T(8,128)S(1)}, f32[16,4,8,8,128]{4,0,3,1,2:T(8,128)}) fusion(f32[16,4,8,8]{0,3,1,2:T(8,128)S(1)} %get-tuple-element.26, f32[8,128,16,4,8]{1,2,4,3,0:T(8,128)S(1)} %get-tuple-element.27, pred[128]{0:T(512)(128)(4,1)S(1)} %add_compare_fusion.1, ...), kind=kLoop, calls=%fused_computation.79 | loop fusion | flops 5234688 | bytes 8454400 | tf_op jit(solution)/shard_map/reduce_sum | solution.py:22
  65.0 0.7 reshape.437
  65.7 4.5 %all-to-all-start.1 = ((f32[16,1,256]{2,1,0:T(1,128)}), f32[16,1,256]{2,1,0:T(1,128)S(1)}, u32[]{:S(2)}, u32[]{:S(2)}) async-start(f32[16,1,256]{2,1,0:T(1,128)} %reshape.437), calls=%async_computation.1 | async-start | bytes 32768 | tf_op jit(solution)/shard_map/all_to_all | solution.py:99
  70.4 3.4 %fusion.11 = f32[16,4,8,8,128]{4,3,1,0,2:T(8,128)S(1)} fusion(bf16[128,8,128,1,1]{0,2,4,3,1:T(8,128)(2,1)S(1)} %bitcast.166, f32[16,4,8,8,128]{4,0,3,1,2:T(8,128)} %get-tuple-element.11), kind=kOutput, calls=%fused_computation.20 | convolution fusion | flops 805306368 | bytes 4456448 | tf_op jit(solution)/shard_map/urpyj,jpi->urpyi/dot_general | solution.py:23
  73.8 3.1 %fusion.14 = f32[16,4,8,8,128]{4,3,1,0,2:T(8,128)} fusion(bf16[128,8,128,1,1]{0,2,4,3,1:T(8,128)(2,1)S(1)} %bitcast.167, f32[16,4,8,8,128]{4,0,3,1,2:T(8,128)S(1)} %copy-done), kind=kOutput, calls=%fused_computation.21 | convolution fusion | flops 805306368 | bytes 4456448 | tf_op jit(solution)/shard_map/urpyj,jpi->urpyi/dot_general | solution.py:23
  77.0 0.7 reshape.439
  77.7 7.2 %all-to-all-start.2 = ((f32[16,1,256]{2,1,0:T(1,128)}), f32[16,1,256]{2,1,0:T(1,128)S(1)}, u32[]{:S(2)}, u32[]{:S(2)}) async-start(f32[16,1,256]{2,1,0:T(1,128)} %reshape.439), calls=%async_computation.2 | async-start | bytes 32768 | tf_op jit(solution)/shard_map/all_to_all | solution.py:100
  84.9 3.4 %fusion.2 = f32[1,16,4,64,128]{4,3,2,0,1:T(8,128)} fusion(f32[16,4,8,8,128]{4,3,1,0,2:T(8,128)} %fusion.14, f32[16,4,8,8,128]{4,3,1,0,2:T(8,128)S(1)} %fusion.11, f32[16,4,64]{2,1,0:T(4,128)S(1)} %copy.119, f32[16,4,64]{2,1,0:T(4,128)S(1)} %copy.114), kind=kLoop, calls=%fused_computation.4 | loop fusion | flops 1572864 | bytes 6324224 | tf_op jit(solution)/shard_map/add | solution.py:80
  88.4 3.9 %all-to-all-done.2 = f32[16,1,256]{2,1,0:T(1,128)S(1)} async-done(((f32[16,1,256]{2,1,0:T(1,128)}), f32[16,1,256]{2,1,0:T(1,128)S(1)}, u32[]{:S(2)}, u32[]{:S(2)}) %all-to-all-start.2) | async-done | bytes 16416 | tf_op jit(solution)/shard_map/all_to_all | solution.py:100
  92.3 3.9 %all-to-all-start = ((f32[1,16,4,64,128]{4,3,2,0,1:T(8,128)}), f32[1,16,4,64,128]{4,3,2,0,1:T(8,128)S(1)}, u32[]{:S(2)}, u32[]{:S(2)}) async-start(f32[1,16,4,64,128]{4,3,2,0,1:T(8,128)} %fusion.2), calls=%async_computation | async-start | bytes 4194304 | tf_op jit(solution)/shard_map/all_to_all | solution.py:98
  96.8 12.8 %fusion.19 = (bf16[260,1024]{1,0:T(8,128)(2,1)S(1)}, bf16[260,1024]{1,0:T(8,128)(2,1)S(1)}) fusion(bf16[1,4,2,1024]{3,2,1,0:T(2,128)(2,1)S(1)} %bitcast.181, bf16[1,256,2,1024]{3,2,1,0:T(2,128)(2,1)} %bitcast.165), kind=kLoop, calls=%fused_computation.28 | loop fusion | flops 2129920 | bytes 2129920 | tf_op jit(solution)/shard_map/slice | solution.py:53
  112.6 0.7 reduce.11
  113.5 31.7 %all-to-all-done = f32[1,16,4,64,128]{4,3,2,0,1:T(8,128)S(1)} async-done(((f32[1,16,4,64,128]{4,3,2,0,1:T(8,128)}), f32[1,16,4,64,128]{4,3,2,0,1:T(8,128)S(1)}, u32[]{:S(2)}, u32[]{:S(2)}) %all-to-all-start) | async-done | bytes 2097184 | tf_op jit(solution)/shard_map/all_to_all | solution.py:98
  145.2 0.7 fusion
  146.4 0.7 copy.133
  (53 shorter events, 6.1 us)
Async XLA Ops:
  6.5 11.6 %copy-start.3 = (s32[32]{0:T(128)S(1)}, s32[32]{0:T(128)}, u32[]{:S(2)}) copy-start(s32[32]{0:T(128)} %param.13) | copy-start | bytes 388
  6.5 50.8 %all-gather.2.cloned.1.call-start = ((), (), s32[]{:S(2)}) async-start(), calls=%async_computation.3 | async-start | bytes 1114112 | tf_op jit(solution)/shard_map/all_gather | solution.py:112
  8.6 18.7 %collective-permute-start = (bf16[1,128,2,1024]{1,3,2,0:T(8,128)(2,1)S(1)}, bf16[1,128,2,1024]{1,3,2,0:T(8,128)(2,1)S(1)}, u32[]{:S(2)}, u32[]{:S(2)}) collective-permute-start(bf16[1,128,2,1024]{1,3,2,0:T(8,128)(2,1)S(1)} %copy.107), channel_id=1, source_target_pairs={{0,496},{16,0},{32,16},{48,32},{64,48},{80,64},{96,80},{112,96},{1... | collective-permute-start | bytes 1572872 | tf_op jit(solution)/shard_map/ppermute | solution.py:15
  65.7 12.0 %all-to-all-start.1 = ((f32[16,1,256]{2,1,0:T(1,128)}), f32[16,1,256]{2,1,0:T(1,128)S(1)}, u32[]{:S(2)}, u32[]{:S(2)}) async-start(f32[16,1,256]{2,1,0:T(1,128)} %reshape.437), calls=%async_computation.1 | async-start | bytes 32768 | tf_op jit(solution)/shard_map/all_to_all | solution.py:99
  70.4 3.4 %copy-start = (f32[16,4,8,8,128]{4,0,3,1,2:T(8,128)S(1)}, f32[16,4,8,8,128]{4,0,3,1,2:T(8,128)}, u32[]{:S(2)}) copy-start(f32[16,4,8,8,128]{4,0,3,1,2:T(8,128)} %get-tuple-element.29) | copy-start | bytes 6291460
  77.7 14.6 %all-to-all-start.2 = ((f32[16,1,256]{2,1,0:T(1,128)}), f32[16,1,256]{2,1,0:T(1,128)S(1)}, u32[]{:S(2)}, u32[]{:S(2)}) async-start(f32[16,1,256]{2,1,0:T(1,128)} %reshape.439), calls=%async_computation.2 | async-start | bytes 32768 | tf_op jit(solution)/shard_map/all_to_all | solution.py:100
  88.4 8.4 %copy-start.2 = (bf16[1,1,4,2,1024]{4,3,2,1,0:T(2,128)(2,1)S(1)}, bf16[1,1,4,2,1024]{4,3,2,1,0:T(2,128)(2,1)}, u32[]{:S(2)}) copy-start(bf16[1,1,4,2,1024]{4,3,2,1,0:T(2,128)(2,1)} %param.8) | copy-start | bytes 49156
  92.3 52.9 %all-to-all-start = ((f32[1,16,4,64,128]{4,3,2,0,1:T(8,128)}), f32[1,16,4,64,128]{4,3,2,0,1:T(8,128)S(1)}, u32[]{:S(2)}, u32[]{:S(2)}) async-start(f32[1,16,4,64,128]{4,3,2,0,1:T(8,128)} %fusion.2), calls=%async_computation | async-start | bytes 4194304 | tf_op jit(solution)/shard_map/all_to_all | solution.py:98
  96.8 13.0 %copy-start.1 = (bf16[1,1,4,8192]{3,2,1,0:T(4,128)(2,1)S(1)}, bf16[1,1,4,8192]{3,2,1,0:T(4,128)(2,1)}, u32[]{:S(2)}) copy-start(bf16[1,1,4,8192]{3,2,1,0:T(4,128)(2,1)} %param.7) | copy-start | bytes 196612
Sparse Core Ops, SparseCore 0:
  9.5 47.8 all-gather.1
where the time goes:
time: 154 us
  waiting for transfers between devices  73.5 us (48%)
  starting transfers between devices  23.7 us (15%)
  other arithmetic  23.6 us (15%)
  between operations  14.4 us (9%)
  matrix products  9.42 us (6%)
  local copies, waits for them, and re-layouts  9.41 us (6%)
    all_to_all x1, waiting for transfers between devices, spread(): lax.all_to_all(partial_sums[0][None], 'sample', split_axis=1, concat_axis...  31.7 us
    all_gather x1, waiting for transfers between devices, per_device(): every_rows = lax.all_gather(queries, 'sample', axis=1, tiled=True)[0]  30 us
    slice x1, other arithmetic, suffix_terms(): joined[:, :, 1].reshape(sample_count, total_len, KVH, HEAD_SIZE)  12.8 us
    ppermute x1, starting transfers between devices, from_behind(): return lax.ppermute(value, axis, pairs)  8.12 us
    all_to_all x1, starting transfers between devices, spread(): lax.all_to_all(partial_sums[2][None], 'sample', split_axis=1, concat_axis...  7.22 us
    ppermute x1, waiting for transfers between devices, from_behind(): return lax.ppermute(value, axis, pairs)  7.22 us
    dot_general x3, matrix products, apply_weights(): jnp.einsum(form, weights, value_matrix, precision=lax.Precision.HIGHEST)  7.01 us
    unnamed x16, local copies, waits for them, and re-layouts  4.55 us
  transfers between devices with their start and end apart: 5, of which 4 were waited for; matrix products, arithmetic and copies ran while one was open for 21% of the time, Pallas kernels for 0%

commit v1 on v0

--- a/solution.py
+++ b/solution.py
@@ -7,6 +7,22 @@
 KVH = 8
 HEAD_SIZE = 128
 NEG = -1e30
+
+
+def gather_around(x, axis, dim):
+    ways, here, lap = (lax.axis_size(axis), lax.axis_index(axis), x.shape[dim])
+    lengths = [n * ways if d == dim else n for d, n in enumerate(x.shape)]
+    full = lax.dynamic_update_slice_in_dim(jnp.zeros(lengths, x.dtype), x, here * lap, axis=dim)
+    going_up = going_down = x
+    for far in range(1, ways // 2 + 1):
+        going_up = lax.ppermute(going_up, axis, [(d, (d + 1) % ways) for d in range(ways)])
+        full = lax.dynamic_update_slice_in_dim(full, going_up, (here - far) % ways * lap, axis=dim)
+        if 2 * far < ways:
+            going_down = lax.ppermute(going_down, axis, [(d, (d - 1) % ways) for d in range(ways)])
+            full = lax.dynamic_update_slice_in_dim(
+                full, going_down, (here + far) % ways * lap, axis=dim
+            )
+    return full
 
 
 def from_behind(value, axis, steps):
@@ -109,7 +125,7 @@
     half_len = block_len * sample_count
     own_length = prefix_len[prompt_row]
     local_rows = queries[0]
-    every_rows = lax.all_gather(queries, "sample", axis=1, tiled=True)[0]
+    every_rows = gather_around(queries, "sample", 1)[0]
     near_part = suffix_terms(local_rows, suffix_kv[0], new_kv[0], suffix_len[0])
     moved = from_behind(prefix_tail, "prompt", -1)
     own_part = prefix_terms(every_rows, prefix_head[0], sample_slot * block_len, own_length)

time: 154 us -> 182 us (1.18)
  local copies, waits for them, and re-layouts: 9.41 us -> 47.5 us
  waiting for transfers between devices: 73.5 us -> 40.8 us
  starting transfers between devices: 23.7 us -> 56 us
  between operations: 14.4 us -> 1.58 us
    dynamic_update_slice x0 -> x16, local copies, waits for them, and re-layouts: none -> 32 us  [the longest x8 16 us: gather_around(): lax.dynamic_update_slice_in_dim(full, going_up, (here - far) % ways * lap...]
    ppermute x0 -> x15, starting transfers between devices: none -> 30.3 us  [the longest x7 26.8 us: gather_around(): lax.ppermute(going_down, axis, [(d, (d - 1) % ways) for d in range(ways)])]
    all_gather x1 -> x0, waiting for transfers between devices: 30 us -> none  [per_device(): every_rows = lax.all_gather(queries, 'sample', axis=1, tiled=True)[0]]
    ppermute x1, waiting for transfers between devices: 7.22 us -> 0.01 us  [from_behind(): return lax.ppermute(value, axis, pairs)]
    ppermute x0 -> x15, waiting for transfers between devices: none -> 4.56 us  [the longest x8 3.91 us: gather_around(): lax.ppermute(going_up, axis, [(d, (d + 1) % ways) for d in range(ways)])]
    all_to_all x1, starting transfers between devices: 4.46 us -> 7.93 us  [spread(): lax.all_to_all(partial_sums[1][None], 'sample', split_axis=1, concat_axis...]
    slice x2, local copies, waits for them, and re-layouts: 0.07 us -> 2.6 us  [prefix_terms(): pairs[:, 1].reshape(block_len, KVH, HEAD_SIZE).astype(jnp.float32)]
    dot_general x2, matrix products: 2.02 us -> 4.53 us  [prefix_terms(): jnp.einsum('rhlxf,vlf->rhlxv', grouped_queries, key_matrix, preferred_ele...]
  transfers between devices with their start and end apart: 5 -> 19, of which waited for: 4 -> 12; matrix products, arithmetic and copies ran while one was open for 21% -> 40% of each run, Pallas kernels for 0% -> 0%
where the time goes in v1:
time: 182 us; the launch traced here: 181 us
  starting transfers between devices  56 us (31%)
  local copies, waits for them, and re-layouts  47.5 us (26%)
  waiting for transfers between devices  40.8 us (22%)
  other arithmetic  24.4 us (13%)
  matrix products  10.9 us (6%)
    all_to_all x1, waiting for transfers between devices, spread(): lax.all_to_all(partial_sums[0][None], 'sample', split_axis=1, concat_axis...  31.6 us
    ppermute x7, starting transfers between devices, gather_around(): lax.ppermute(going_down, axis, [(d, (d - 1) % ways) for d in range(ways)])  26.8 us
    dynamic_update_slice x8, local copies, waits for them, and re-layouts, gather_around(): lax.dynamic_update_slice_in_dim(full, going_up, (here - far) % ways * lap...  16 us
    dynamic_update_slice x7, local copies, waits for them, and re-layouts, gather_around(): lax.dynamic_update_slice_in_dim(full, going_down, (here + far) % ways * l...  14 us
    slice x1, other arithmetic, suffix_terms(): joined[:, :, 1].reshape(sample_count, total_len, KVH, HEAD_SIZE)  12.8 us
    all_to_all x1, starting transfers between devices, spread(): lax.all_to_all(partial_sums[1][None], 'sample', split_axis=1, concat_axis...  7.93 us
    ppermute x1, starting transfers between devices, from_behind(): return lax.ppermute(value, axis, pairs)  7.28 us
    all_to_all x1, starting transfers between devices, spread(): lax.all_to_all(partial_sums[2][None], 'sample', split_axis=1, concat_axis...  6.6 us
  transfers between devices with their start and end apart: 19, of which 12 were waited for; matrix products, arithmetic and copies ran while one was open for 40% of the time, Pallas kernels for 0%

profile of v1, /device:TPU:1, one launch (start us, length us, event | category | flops | bytes accessed | tf_op | source)
XLA Modules:
  0.0 181.2 jit_solution(17467634662229346618)
XLA Ops:
  0.0 3.5 %collective-permute-start = (bf16[1,1,4,8192]{3,2,1,0:T(4,128)(2,1)}, bf16[1,1,4,8192]{3,2,1,0:T(4,128)(2,1)S(1)}, u32[]{:S(2)}, u32[]{:S(2)}) collective-permute-start(bf16[1,1,4,8192]{3,2,1,0:T(4,128)(2,1)} %param.7), channel_id=1, source_target_pairs={{0,1},{1,2},{2,3},{3,4},{4,5},{5,6},{6,7},{7,8},{8,9},{9,10},{10,1... | collective-permute-start | bytes 196616 | tf_op jit(solution)/shard_map/ppermute | solution.py:18
  3.5 3.4 %collective-permute-start.1 = (bf16[1,1,4,8192]{3,2,1,0:T(4,128)(2,1)}, bf16[1,1,4,8192]{3,2,1,0:T(4,128)(2,1)S(1)}, u32[]{:S(2)}, u32[]{:S(2)}) collective-permute-start(bf16[1,1,4,8192]{3,2,1,0:T(4,128)(2,1)} %param.7), channel_id=1, source_target_pairs={{0,15},{1,0},{2,1},{3,2},{4,3},{5,4},{6,5},{7,6},{8,7},{9,8},{10,9... | collective-permute-start | bytes 196616 | tf_op jit(solution)/shard_map/ppermute | solution.py:21
  8.0 4.2 %collective-permute-start.3 = (bf16[1,1,4,8192]{3,2,1,0:T(4,128)(2,1)S(1)}, bf16[1,1,4,8192]{3,2,1,0:T(4,128)(2,1)S(1)}, u32[]{:S(2)}, u32[]{:S(2)}) collective-permute-start(bf16[1,1,4,8192]{3,2,1,0:T(4,128)(2,1)S(1)} %collective-permute-done.1), channel_id=1, source_target_pairs={{0,15},{1,0},{2,1},{3,2},{4,3},{5,4},{6,5},{7,6},{8,7},{9,8},{10,9... | collective-permute-start | bytes 196616 | tf_op jit(solution)/shard_map/ppermute | solution.py:21
  13.1 4.0 %collective-permute-start.5 = (bf16[1,1,4,8192]{3,2,1,0:T(4,128)(2,1)S(1)}, bf16[1,1,4,8192]{3,2,1,0:T(4,128)(2,1)S(1)}, u32[]{:S(2)}, u32[]{:S(2)}) collective-permute-start(bf16[1,1,4,8192]{3,2,1,0:T(4,128)(2,1)S(1)} %collective-permute-done.3), channel_id=1, source_target_pairs={{0,15},{1,0},{2,1},{3,2},{4,3},{5,4},{6,5},{7,6},{8,7},{9,8},{10,9... | collective-permute-start | bytes 196616 | tf_op jit(solution)/shard_map/ppermute | solution.py:21
  18.0 4.0 %collective-permute-start.7 = (bf16[1,1,4,8192]{3,2,1,0:T(4,128)(2,1)S(1)}, bf16[1,1,4,8192]{3,2,1,0:T(4,128)(2,1)S(1)}, u32[]{:S(2)}, u32[]{:S(2)}) collective-permute-start(bf16[1,1,4,8192]{3,2,1,0:T(4,128)(2,1)S(1)} %collective-permute-done.5), channel_id=1, source_target_pairs={{0,15},{1,0},{2,1},{3,2},{4,3},{5,4},{6,5},{7,6},{8,7},{9,8},{10,9... | collective-permute-start | bytes 196616 | tf_op jit(solution)/shard_map/ppermute | solution.py:21
  22.9 4.0 %collective-permute-start.9 = (bf16[1,1,4,8192]{3,2,1,0:T(4,128)(2,1)S(1)}, bf16[1,1,4,8192]{3,2,1,0:T(4,128)(2,1)S(1)}, u32[]{:S(2)}, u32[]{:S(2)}) collective-permute-start(bf16[1,1,4,8192]{3,2,1,0:T(4,128)(2,1)S(1)} %collective-permute-done.7), channel_id=1, source_target_pairs={{0,15},{1,0},{2,1},{3,2},{4,3},{5,4},{6,5},{7,6},{8,7},{9,8},{10,9... | collective-permute-start | bytes 196616 | tf_op jit(solution)/shard_map/ppermute | solution.py:21
  29.7 7.3 %collective-permute-start.15 = (bf16[1,128,2,1024]{1,3,2,0:T(8,128)(2,1)}, bf16[1,128,2,1024]{1,3,2,0:T(8,128)(2,1)}, u32[]{:S(2)}, u32[]{:S(2)}) collective-permute-start(bf16[1,128,2,1024]{1,3,2,0:T(8,128)(2,1)} %copy.155), channel_id=1, source_target_pairs={{0,496},{16,0},{32,16},{48,32},{64,48},{80,64},{96,80},{112,96},{1... | collective-permute-start | bytes 1572872 | tf_op jit(solution)/shard_map/ppermute | solution.py:31
  38.4 4.4 %collective-permute-start.11 = (bf16[1,1,4,8192]{3,2,1,0:T(4,128)(2,1)S(1)}, bf16[1,1,4,8192]{3,2,1,0:T(4,128)(2,1)S(1)}, u32[]{:S(2)}, u32[]{:S(2)}) collective-permute-start(bf16[1,1,4,8192]{3,2,1,0:T(4,128)(2,1)S(1)} %collective-permute-done.9), channel_id=1, source_target_pairs={{0,15},{1,0},{2,1},{3,2},{4,3},{5,4},{6,5},{7,6},{8,7},{9,8},{10,9... | collective-permute-start | bytes 196616 | tf_op jit(solution)/shard_map/ppermute | solution.py:21
  44.7 2.0 %dynamic_update_slice.48 = bf16[1,16,4,8192]{3,1,2,0:T(8,128)(2,1)S(1)} dynamic-update-slice(bf16[1,16,4,8192]{3,1,2,0:T(8,128)(2,1)S(1)} %broadcast_in_dim.71, bf16[1,1,4,8192]{3,1,2,0:T(2,128)(2,1)S(1)} %copy.133, s32[]{:T(128)} %constant.102.clone.1, s32[]{:T(128)S(6)} %select_n.141, s32[]{:T(128)} %constant.102.clone.1, s32[]{:T(128)} %constant.102.clone.1) | dynamic-update-slice | bytes 131076 | tf_op jit(solution)/shard_map/dynamic_update_slice | solution.py:15
  46.7 2.7 %collective-permute-start.13 = (bf16[1,1,4,8192]{3,2,1,0:T(4,128)(2,1)S(1)}, bf16[1,1,4,8192]{3,2,1,0:T(4,128)(2,1)S(1)}, u32[]{:S(2)}, u32[]{:S(2)}) collective-permute-start(bf16[1,1,4,8192]{3,2,1,0:T(4,128)(2,1)S(1)} %collective-permute-done.11), channel_id=1, source_target_pairs={{0,15},{1,0},{2,1},{3,2},{4,3},{5,4},{6,5},{7,6},{8,7},{9,8},{10,9... | collective-permute-start | bytes 196616 | tf_op jit(solution)/shard_map/ppermute | solution.py:21
  50.2 2.0 %dynamic_update_slice.49 = bf16[1,16,4,8192]{3,1,2,0:T(8,128)(2,1)S(1)} dynamic-update-slice(bf16[1,16,4,8192]{3,1,2,0:T(8,128)(2,1)S(1)} %dynamic_update_slice.48, bf16[1,1,4,8192]{3,1,2,0:T(2,128)(2,1)S(1)} %copy.134, s32[]{:T(128)} %constant.102.clone.1, s32[]{:T(128)S(6)} %select_n.143, s32[]{:T(128)} %constant.102.clone.1, s32[]{:T(128)} %constant.102.clone.1) | dynamic-update-slice | bytes 131076 | tf_op jit(solution)/shard_map/dynamic_update_slice | solution.py:19
  52.3 2.0 %dynamic_update_slice.50 = bf16[1,16,4,8192]{3,1,2,0:T(8,128)(2,1)S(1)} dynamic-update-slice(bf16[1,16,4,8192]{3,1,2,0:T(8,128)(2,1)S(1)} %dynamic_update_slice.49, bf16[1,1,4,8192]{3,1,2,0:T(2,128)(2,1)S(1)} %copy.135, s32[]{:T(128)} %constant.102.clone.1, s32[]{:T(128)S(6)} %select_n.145, s32[]{:T(128)} %constant.102.clone.1, s32[]{:T(128)} %constant.102.clone.1) | dynamic-update-slice | bytes 131076 | tf_op jit(solution)/shard_map/dynamic_update_slice | solution.py:22
  84.1 2.1 %fusion.7 = f32[16,4,8,8]{3,1,0,2:T(4,128)} fusion(f32[8,16,4,8,128]{4,3,2,1,0:T(8,128)S(1)} %get-tuple-element.23, f32[16,4,8,8]{3,1,0,2:T(4,128)S(1)} %get-tuple-element.22, pred[128]{0:T(512)(128)(4,1)S(1)} %get-tuple-element.25), kind=kLoop, calls=%fused_computation.18 | loop fusion | flops 2617344 | bytes 2130048 | tf_op jit(solution)/shard_map/reduce_sum | solution.py:38
  89.7 2.7 %bitcast_reduce_fusion = (f32[16,4,8,8]{3,1,0,2:T(4,128)}, f32[8,16,4,8,128]{4,3,2,1,0:T(8,128)}) fusion(pred[128]{0:T(512)(128)(4,1)S(1)} %get-tuple-element.24, bf16[128,8,128,1,1]{0,2,4,3,1:T(8,128)(2,1)S(1)} %bitcast.176, bf16[16,4,8,8,128]{4,3,2,0,1:T(8,128)(2,1)S(1)} %bitcast.165), kind=kOutput, calls=%fused_computation.6 | convolution fusion | flops 135786496 | bytes 3424384 | tf_op jit(solution)/shard_map/rhlxf,vlf->rhlxv/dot_general | solution.py:54
  93.5 2.6 %fusion.9 = f32[16,4,8,8]{3,1,0,2:T(4,128)S(1)} fusion(f32[8,16,4,8,128]{4,3,2,1,0:T(8,128)} %get-tuple-element.21, f32[16,4,8,8]{3,1,0,2:T(4,128)} %get-tuple-element.20, pred[128]{0:T(512)(128)(4,1)S(1)} %get-tuple-element.24), kind=kLoop, calls=%fused_computation.19 | loop fusion | flops 2617344 | bytes 2130048 | tf_op jit(solution)/shard_map/reduce_sum | solution.py:38
  97.2 7.9 %all-to-all-start.1 = ((f32[16,1,256]{2,1,0:T(1,128)}), f32[16,1,256]{2,1,0:T(1,128)S(1)}, u32[]{:S(2)}, u32[]{:S(2)}) async-start(f32[16,1,256]{2,1,0:T(1,128)} %reshape.436), calls=%async_computation.1 | async-start | bytes 32768 | tf_op jit(solution)/shard_map/all_to_all | solution.py:115
  105.3 2.7 %convolution_bitcast_fusion.1 = f32[16,4,8,8,128]{4,3,1,0,2:T(8,128)} fusion(bf16[128,8,128,1,1]{0,2,4,3,1:T(8,128)(2,1)S(1)} %bitcast.181, f32[8,16,4,8,128]{4,3,2,1,0:T(8,128)S(1)} %get-tuple-element.23, f32[16,4,8,8]{3,1,0,2:T(4,128)S(1)} %get-tuple-element.22, pred[128]{0:T(512)(128)(4,1)S(1)} %get-tuple-element.25), kind=kOutput, calls=%fused_computation.17 | convolution fusion | flops 807403520 | bytes 4472960 | tf_op jit(solution)/shard_map/urpyj,jpi->urpyi/dot_general | solution.py:39
  108.0 2.7 %convolution_bitcast_fusion = f32[16,4,8,8,128]{4,3,1,0,2:T(8,128)} fusion(bf16[128,8,128,1,1]{0,2,4,3,1:T(8,128)(2,1)S(1)} %bitcast.182, f32[8,16,4,8,128]{4,3,2,1,0:T(8,128)S(1)} %copy-done, f32[16,4,8,8]{3,1,0,2:T(4,128)S(1)} %copy-done.1, pred[128]{0:T(512)(128)(4,1)S(1)} %get-tuple-element.24), kind=kOutput, calls=%fused_computation.16 | convolution fusion | flops 807403520 | bytes 4472960 | tf_op jit(solution)/shard_map/urpyj,jpi->urpyi/dot_general | solution.py:39
  112.4 6.6 %all-to-all-start.2 = ((f32[16,1,256]{2,1,0:T(1,128)}), f32[16,1,256]{2,1,0:T(1,128)S(1)}, u32[]{:S(2)}, u32[]{:S(2)}) async-start(f32[16,1,256]{2,1,0:T(1,128)} %reshape.438), calls=%async_computation.2 | async-start | bytes 32768 | tf_op jit(solution)/shard_map/all_to_all | solution.py:116
  119.0 3.5 %fusion.2 = f32[1,16,4,64,128]{4,3,2,0,1:T(8,128)} fusion(f32[16,4,8,8,128]{4,3,1,0,2:T(8,128)} %convolution_bitcast_fusion, f32[16,4,8,8,128]{4,3,1,0,2:T(8,128)S(1)} %copy-done.2, f32[16,4,64]{2,1,0:T(4,128)S(1)} %copy.166, f32[16,4,64]{2,1,0:T(4,128)S(1)} %copy.162), kind=kLoop, calls=%fused_computation.4 | loop fusion | flops 1572864 | bytes 6324224 | tf_op jit(solution)/shard_map/add | solution.py:96
  122.5 3.8 %all-to-all-done.2 = f32[16,1,256]{2,1,0:T(1,128)S(1)} async-done(((f32[16,1,256]{2,1,0:T(1,128)}), f32[16,1,256]{2,1,0:T(1,128)S(1)}, u32[]{:S(2)}, u32[]{:S(2)}) %all-to-all-start.2) | async-done | bytes 16416 | tf_op jit(solution)/shard_map/all_to_all | solution.py:116
  126.4 3.9 %all-to-all-start = ((f32[1,16,4,64,128]{4,3,2,0,1:T(8,128)}), f32[1,16,4,64,128]{4,3,2,0,1:T(8,128)S(1)}, u32[]{:S(2)}, u32[]{:S(2)}) async-start(f32[1,16,4,64,128]{4,3,2,0,1:T(8,128)} %fusion.2), calls=%async_computation | async-start | bytes 4194304 | tf_op jit(solution)/shard_map/all_to_all | solution.py:114
  130.9 12.8 %fusion.13 = (bf16[260,1024]{1,0:T(8,128)(2,1)S(1)}, bf16[260,1024]{1,0:T(8,128)(2,1)S(1)}) fusion(bf16[1,4,2,1024]{3,2,1,0:T(2,128)(2,1)S(1)} %bitcast.186, bf16[1,256,2,1024]{3,2,1,0:T(2,128)(2,1)} %bitcast.174), kind=kLoop, calls=%fused_computation.26 | loop fusion | flops 2129920 | bytes 2129920 | tf_op jit(solution)/shard_map/slice | solution.py:69
  147.6 31.6 %all-to-all-done = f32[1,16,4,64,128]{4,3,2,0,1:T(8,128)S(1)} async-done(((f32[1,16,4,64,128]{4,3,2,0,1:T(8,128)}), f32[1,16,4,64,128]{4,3,2,0,1:T(8,128)S(1)}, u32[]{:S(2)}, u32[]{:S(2)}) %all-to-all-start) | async-done | bytes 2097184 | tf_op jit(solution)/shard_map/all_to_all | solution.py:114
  (127 shorter events, 53.1 us)
Async XLA Ops:
  0.0 43.7 %copy-start.6 = (bf16[1,1,4,8192]{3,2,1,0:T(4,128)(2,1)S(1)}, bf16[1,1,4,8192]{3,2,1,0:T(4,128)(2,1)}, u32[]{:S(2)}) copy-start(bf16[1,1,4,8192]{3,2,1,0:T(4,128)(2,1)} %param.7) | copy-start | bytes 196612
  0.0 44.0 %copy-start.9 = (s32[32]{0:T(128)S(1)}, s32[32]{0:T(128)}, u32[]{:S(2)}) copy-start(s32[32]{0:T(128)} %param.13) | copy-start | bytes 388
  0.0 7.8 %collective-permute-start = (bf16[1,1,4,8192]{3,2,1,0:T(4,128)(2,1)}, bf16[1,1,4,8192]{3,2,1,0:T(4,128)(2,1)S(1)}, u32[]{:S(2)}, u32[]{:S(2)}) collective-permute-start(bf16[1,1,4,8192]{3,2,1,0:T(4,128)(2,1)} %param.7), channel_id=1, source_target_pairs={{0,1},{1,2},{2,3},{3,4},{4,5},{5,6},{6,7},{7,8},{8,9},{9,10},{10,1... | collective-permute-start | bytes 196616 | tf_op jit(solution)/shard_map/ppermute | solution.py:18
  3.5 4.5 %collective-permute-start.1 = (bf16[1,1,4,8192]{3,2,1,0:T(4,128)(2,1)}, bf16[1,1,4,8192]{3,2,1,0:T(4,128)(2,1)S(1)}, u32[]{:S(2)}, u32[]{:S(2)}) collective-permute-start(bf16[1,1,4,8192]{3,2,1,0:T(4,128)(2,1)} %param.7), channel_id=1, source_target_pairs={{0,15},{1,0},{2,1},{3,2},{4,3},{5,4},{6,5},{7,6},{8,7},{9,8},{10,9... | collective-permute-start | bytes 196616 | tf_op jit(solution)/shard_map/ppermute | solution.py:21
  7.8 5.1 %collective-permute-start.2 = (bf16[1,1,4,8192]{3,2,1,0:T(4,128)(2,1)S(1)}, bf16[1,1,4,8192]{3,2,1,0:T(4,128)(2,1)S(1)}, u32[]{:S(2)}, u32[]{:S(2)}) collective-permute-start(bf16[1,1,4,8192]{3,2,1,0:T(4,128)(2,1)S(1)} %collective-permute-done), channel_id=1, source_target_pairs={{0,1},{1,2},{2,3},{3,4},{4,5},{5,6},{6,7},{7,8},{8,9},{9,10},{10,1... | collective-permute-start | bytes 196616 | tf_op jit(solution)/shard_map/ppermute | solution.py:18
  8.0 5.1 %collective-permute-start.3 = (bf16[1,1,4,8192]{3,2,1,0:T(4,128)(2,1)S(1)}, bf16[1,1,4,8192]{3,2,1,0:T(4,128)(2,1)S(1)}, u32[]{:S(2)}, u32[]{:S(2)}) collective-permute-start(bf16[1,1,4,8192]{3,2,1,0:T(4,128)(2,1)S(1)} %collective-permute-done.1), channel_id=1, source_target_pairs={{0,15},{1,0},{2,1},{3,2},{4,3},{5,4},{6,5},{7,6},{8,7},{9,8},{10,9... | collective-permute-start | bytes 196616 | tf_op jit(solution)/shard_map/ppermute | solution.py:21
  13.0 4.9 %collective-permute-start.4 = (bf16[1,1,4,8192]{3,2,1,0:T(4,128)(2,1)S(1)}, bf16[1,1,4,8192]{3,2,1,0:T(4,128)(2,1)S(1)}, u32[]{:S(2)}, u32[]{:S(2)}) collective-permute-start(bf16[1,1,4,8192]{3,2,1,0:T(4,128)(2,1)S(1)} %collective-permute-done.2), channel_id=1, source_target_pairs={{0,1},{1,2},{2,3},{3,4},{4,5},{5,6},{6,7},{7,8},{8,9},{9,10},{10,1... | collective-permute-start | bytes 196616 | tf_op jit(solution)/shard_map/ppermute | solution.py:18
  13.1 4.9 %collective-permute-start.5 = (bf16[1,1,4,8192]{3,2,1,0:T(4,128)(2,1)S(1)}, bf16[1,1,4,8192]{3,2,1,0:T(4,128)(2,1)S(1)}, u32[]{:S(2)}, u32[]{:S(2)}) collective-permute-start(bf16[1,1,4,8192]{3,2,1,0:T(4,128)(2,1)S(1)} %collective-permute-done.3), channel_id=1, source_target_pairs={{0,15},{1,0},{2,1},{3,2},{4,3},{5,4},{6,5},{7,6},{8,7},{9,8},{10,9... | collective-permute-start | bytes 196616 | tf_op jit(solution)/shard_map/ppermute | solution.py:21
  17.9 4.9 %collective-permute-start.6 = (bf16[1,1,4,8192]{3,2,1,0:T(4,128)(2,1)S(1)}, bf16[1,1,4,8192]{3,2,1,0:T(4,128)(2,1)S(1)}, u32[]{:S(2)}, u32[]{:S(2)}) collective-permute-start(bf16[1,1,4,8192]{3,2,1,0:T(4,128)(2,1)S(1)} %collective-permute-done.4), channel_id=1, source_target_pairs={{0,1},{1,2},{2,3},{3,4},{4,5},{5,6},{6,7},{7,8},{8,9},{9,10},{10,1... | collective-permute-start | bytes 196616 | tf_op jit(solution)/shard_map/ppermute | solution.py:18
  18.0 4.9 %collective-permute-start.7 = (bf16[1,1,4,8192]{3,2,1,0:T(4,128)(2,1)S(1)}, bf16[1,1,4,8192]{3,2,1,0:T(4,128)(2,1)S(1)}, u32[]{:S(2)}, u32[]{:S(2)}) collective-permute-start(bf16[1,1,4,8192]{3,2,1,0:T(4,128)(2,1)S(1)} %collective-permute-done.5), channel_id=1, source_target_pairs={{0,15},{1,0},{2,1},{3,2},{4,3},{5,4},{6,5},{7,6},{8,7},{9,8},{10,9... | collective-permute-start | bytes 196616 | tf_op jit(solution)/shard_map/ppermute | solution.py:21
  22.8 4.9 %collective-permute-start.8 = (bf16[1,1,4,8192]{3,2,1,0:T(4,128)(2,1)S(1)}, bf16[1,1,4,8192]{3,2,1,0:T(4,128)(2,1)S(1)}, u32[]{:S(2)}, u32[]{:S(2)}) collective-permute-start(bf16[1,1,4,8192]{3,2,1,0:T(4,128)(2,1)S(1)} %collective-permute-done.6), channel_id=1, source_target_pairs={{0,1},{1,2},{2,3},{3,4},{4,5},{5,6},{6,7},{7,8},{8,9},{9,10},{10,1... | collective-permute-start | bytes 196616 | tf_op jit(solution)/shard_map/ppermute | solution.py:18
  22.9 15.4 %collective-permute-start.9 = (bf16[1,1,4,8192]{3,2,1,0:T(4,128)(2,1)S(1)}, bf16[1,1,4,8192]{3,2,1,0:T(4,128)(2,1)S(1)}, u32[]{:S(2)}, u32[]{:S(2)}) collective-permute-start(bf16[1,1,4,8192]{3,2,1,0:T(4,128)(2,1)S(1)} %collective-permute-done.7), channel_id=1, source_target_pairs={{0,15},{1,0},{2,1},{3,2},{4,3},{5,4},{6,5},{7,6},{8,7},{9,8},{10,9... | collective-permute-start | bytes 196616 | tf_op jit(solution)/shard_map/ppermute | solution.py:21
  27.7 15.1 %collective-permute-start.10 = (bf16[1,1,4,8192]{3,2,1,0:T(4,128)(2,1)S(1)}, bf16[1,1,4,8192]{3,2,1,0:T(4,128)(2,1)S(1)}, u32[]{:S(2)}, u32[]{:S(2)}) collective-permute-start(bf16[1,1,4,8192]{3,2,1,0:T(4,128)(2,1)S(1)} %collective-permute-done.8), channel_id=1, source_target_pairs={{0,1},{1,2},{2,3},{3,4},{4,5},{5,6},{6,7},{7,8},{8,9},{9,10},{10,1... | collective-permute-start | bytes 196616 | tf_op jit(solution)/shard_map/ppermute | solution.py:18
  29.7 58.2 %collective-permute-start.15 = (bf16[1,128,2,1024]{1,3,2,0:T(8,128)(2,1)}, bf16[1,128,2,1024]{1,3,2,0:T(8,128)(2,1)}, u32[]{:S(2)}, u32[]{:S(2)}) collective-permute-start(bf16[1,128,2,1024]{1,3,2,0:T(8,128)(2,1)} %copy.155), channel_id=1, source_target_pairs={{0,496},{16,0},{32,16},{48,32},{64,48},{80,64},{96,80},{112,96},{1... | collective-permute-start | bytes 1572872 | tf_op jit(solution)/shard_map/ppermute | solution.py:31
  38.4 8.4 %collective-permute-start.11 = (bf16[1,1,4,8192]{3,2,1,0:T(4,128)(2,1)S(1)}, bf16[1,1,4,8192]{3,2,1,0:T(4,128)(2,1)S(1)}, u32[]{:S(2)}, u32[]{:S(2)}) collective-permute-start(bf16[1,1,4,8192]{3,2,1,0:T(4,128)(2,1)S(1)} %collective-permute-done.9), channel_id=1, source_target_pairs={{0,15},{1,0},{2,1},{3,2},{4,3},{5,4},{6,5},{7,6},{8,7},{9,8},{10,9... | collective-permute-start | bytes 196616 | tf_op jit(solution)/shard_map/ppermute | solution.py:21
  42.8 6.6 %collective-permute-start.12 = (bf16[1,1,4,8192]{3,2,1,0:T(4,128)(2,1)S(1)}, bf16[1,1,4,8192]{3,2,1,0:T(4,128)(2,1)S(1)}, u32[]{:S(2)}, u32[]{:S(2)}) collective-permute-start(bf16[1,1,4,8192]{3,2,1,0:T(4,128)(2,1)S(1)} %collective-permute-done.10), channel_id=1, source_target_pairs={{0,1},{1,2},{2,3},{3,4},{4,5},{5,6},{6,7},{7,8},{8,9},{9,10},{10,1... | collective-permute-start | bytes 196616 | tf_op jit(solution)/shard_map/ppermute | solution.py:18
  46.7 30.9 %collective-permute-start.13 = (bf16[1,1,4,8192]{3,2,1,0:T(4,128)(2,1)S(1)}, bf16[1,1,4,8192]{3,2,1,0:T(4,128)(2,1)S(1)}, u32[]{:S(2)}, u32[]{:S(2)}) collective-permute-start(bf16[1,1,4,8192]{3,2,1,0:T(4,128)(2,1)S(1)} %collective-permute-done.11), channel_id=1, source_target_pairs={{0,15},{1,0},{2,1},{3,2},{4,3},{5,4},{6,5},{7,6},{8,7},{9,8},{10,9... | collective-permute-start | bytes 196616 | tf_op jit(solution)/shard_map/ppermute | solution.py:21
  49.4 30.3 %collective-permute-start.14 = (bf16[1,1,4,8192]{3,2,1,0:T(4,128)(2,1)S(1)}, bf16[1,1,4,8192]{3,2,1,0:T(4,128)(2,1)S(1)}, u32[]{:S(2)}, u32[]{:S(2)}) collective-permute-start(bf16[1,1,4,8192]{3,2,1,0:T(4,128)(2,1)S(1)} %collective-permute-done.12), channel_id=1, source_target_pairs={{0,1},{1,2},{2,3},{3,4},{4,5},{5,6},{6,7},{7,8},{8,9},{9,10},{10,1... | collective-permute-start | bytes 196616 | tf_op jit(solution)/shard_map/ppermute | solution.py:18
  93.5 11.7 %copy-start.4 = (bf16[128,1,1024]{0,2,1:T(8,128)(2,1)S(1)}, bf16[128,1,1024]{0,2,1:T(8,128)(2,1)}, u32[]{:S(2)}) copy-start(bf16[128,1,1024]{0,2,1:T(8,128)(2,1)} %get-tuple-element.10) | copy-start | bytes 786436
  97.2 15.3 %all-to-all-start.1 = ((f32[16,1,256]{2,1,0:T(1,128)}), f32[16,1,256]{2,1,0:T(1,128)S(1)}, u32[]{:S(2)}, u32[]{:S(2)}) async-start(f32[16,1,256]{2,1,0:T(1,128)} %reshape.436), calls=%async_computation.1 | async-start | bytes 32768 | tf_op jit(solution)/shard_map/all_to_all | solution.py:115
  108.0 11.0 %copy-start.2 = (f32[16,4,8,8,128]{4,3,1,0,2:T(8,128)S(1)}, f32[16,4,8,8,128]{4,3,1,0,2:T(8,128)}, u32[]{:S(2)}) copy-start(f32[16,4,8,8,128]{4,3,1,0,2:T(8,128)} %convolution_bitcast_fusion.1) | copy-start | bytes 6291460
  112.4 13.9 %all-to-all-start.2 = ((f32[16,1,256]{2,1,0:T(1,128)}), f32[16,1,256]{2,1,0:T(1,128)S(1)}, u32[]{:S(2)}, u32[]{:S(2)}) async-start(f32[16,1,256]{2,1,0:T(1,128)} %reshape.438), calls=%async_computation.2 | async-start | bytes 32768 | tf_op jit(solution)/shard_map/all_to_all | solution.py:116
  126.4 52.9 %all-to-all-start = ((f32[1,16,4,64,128]{4,3,2,0,1:T(8,128)}), f32[1,16,4,64,128]{4,3,2,0,1:T(8,128)S(1)}, u32[]{:S(2)}, u32[]{:S(2)}) async-start(f32[1,16,4,64,128]{4,3,2,0,1:T(8,128)} %fusion.2), calls=%async_computation | async-start | bytes 4194304 | tf_op jit(solution)/shard_map/all_to_all | solution.py:114
  130.9 13.0 %copy-start.7 = (bf16[1,1,4,8192]{3,2,1,0:T(4,128)(2,1)S(1)}, bf16[1,1,4,8192]{3,2,1,0:T(4,128)(2,1)}, u32[]{:S(2)}) copy-start(bf16[1,1,4,8192]{3,2,1,0:T(4,128)(2,1)} %param.7) | copy-start | bytes 196612
  (5 other events, 20.6 us)
